TPU v7x, 256 devices: a whole 4x4x8 slice. The times are simulated.
256 devices in a mesh: dp: 64 (over z, y, core), mp: 4 (over x).
Axes of the slice: x: 4, y: 4, z: 8, core: 2. Of those that a mesh axis runs over, the one named last changes fastest.
Arguments:
- tree_query: bfloat16 [8192, 2048], P('dp', 'mp'), may hold values from -6 to 6
- new_kv: bfloat16 [8192, 2, 512], P('dp', None, 'mp'), may hold values from -6 to 6
- kv_cache: bfloat16 [2560, 2, 128, 512], P('dp', None, None, 'mp'), may hold values from -4 to 4
- page_table: int32 [128, 32], P('dp'), may hold values from 0 to 39, as said below
- cache_len: int32 [128], P('dp'), may hold values from 2 to 4096, as said below
- tree_mask: int32 [128, 64, 64], P('dp'), may hold values from 0 to 1, as said below
- out_weight: bfloat16 [2048, 2048], P('mp'), may hold values from -0.5 to 0.5
- residual_in: bfloat16 [8192, 2048], P('dp'), may hold values from -3 to 3
- norm_gain: float32 [2048], replicated, may hold values from 0.25 to 1.75
- route_ids: int32 [8192, 6], P('dp'), may hold values from 0 to 63, all different within a row; in each aligned block of 128 rows (0 to 127, 128 to 255, ...) at most 16 rows name the same one
- route_weight: float32 [8192, 6], P('dp'), may hold values from 0.05 to 0.5
- w_gate: bfloat16 [64, 2048, 1408], P('dp', None, 'mp'), may hold values from -0.125 to 0.125
- w_up: bfloat16 [64, 2048, 1408], P('dp', None, 'mp'), may hold values from -0.125 to 0.125
- w_down: bfloat16 [64, 1408, 2048], P('dp', None, 'mp'), may hold values from -0.15625 to 0.15625
- shared_gate: bfloat16 [2048, 2816], P('dp', 'mp'), may hold values from -0.125 to 0.125
- shared_up: bfloat16 [2048, 2816], P('dp', 'mp'), may hold values from -0.125 to 0.125
- shared_down: bfloat16 [2816, 2048], P('mp', 'dp'), may hold values from -0.109375 to 0.109375
Outputs:
- layer_out: bfloat16 [8192, 2048], P('dp', 'mp')
Inputs may be any that keep to these rules, and one draw needn't show every extreme that they name: `route_ids`: each row names 6 different experts. Within the rows of one index of dp (aligned blocks of 128 rows) no expert is named by more than 16 rows, and in some block one expert is named by exactly 16 rows. `cache_len`: the pages of the requests of one index of dp number at most 40 together; some request has exactly 4096 cached positions. `page_table`: entry [r, j] is the slot, in the pool of the index of dp that holds request r, of the page with cache positions j * 128 to j * 128 + 127. Entries with j * 128 < cache_len[r] are distinct over the requests of one index of dp; the other entries are valid slots whose contents are not read. tree_mask[r, i, u] is 1 where tree node u is node i or an ancestor of it, else 0; node 0 is the root and each other node's parent has a smaller index.
All inputs are finite; a program needn't handle non-finite values.
Results may differ from a plain program's by a relative error of at most 0.009.
Values may be sent and summed in bfloat16 or wider, within the bound.
No kernel may reach another device: no remote copies, remote signals or barrier semaphores. Data moves between devices by JAX's collectives and lax.ppermute only.
A program may use at most 128 MiB of HBM per device.

v0:
```python
import jax
import jax.numpy as jnp
from jax import lax
from jax.sharding import PartitionSpec as P

NEGATIVE_FILL = -1e30
EPSILON = 1e-05


def normalize(rows, gain):
    values = rows.astype(jnp.float32)
    mean_square = jnp.mean(values * values, axis=-1, keepdims=True)
    return (values * lax.rsqrt(mean_square + EPSILON) * gain).astype(jnp.bfloat16)


def attend_requests(
    queries, tree_keys, tree_values, tree_allow, kv_cache, page_table, cache_len, score_scale
):

    def per_request(request_item):
        q_rows, own_keys, own_values, allow_rows, table_row, length = request_item
        kv_pages = kv_cache[table_row]
        cache_keys = kv_pages[:, 0].reshape(-1, kv_pages.shape[-1])
        cache_values = kv_pages[:, 1].reshape(-1, kv_pages.shape[-1])
        live_mask = (jnp.arange(cache_keys.shape[0], dtype=jnp.int32) < length)[None, :]
        cache_scores = (
            jnp.einsum("qd,kd->qk", q_rows, cache_keys, preferred_element_type=jnp.float32)
            * score_scale
        )
        cache_scores = jnp.where(live_mask, cache_scores, NEGATIVE_FILL)
        tree_scores = (
            jnp.einsum("qd,ud->qu", q_rows, own_keys, preferred_element_type=jnp.float32)
            * score_scale
        )
        tree_scores = jnp.where(allow_rows, tree_scores, NEGATIVE_FILL)
        row_peak = jnp.maximum(jnp.max(cache_scores, axis=1), jnp.max(tree_scores, axis=1))[:, None]
        cache_probs = jnp.where(live_mask, jnp.exp(cache_scores - row_peak), 0.0)
        tree_probs = jnp.where(allow_rows, jnp.exp(tree_scores - row_peak), 0.0)
        denom_sum = jnp.sum(cache_probs, axis=1) + jnp.sum(tree_probs, axis=1)
        weighted = jnp.dot(
            cache_probs.astype(jnp.bfloat16), cache_values, preferred_element_type=jnp.float32
        )
        weighted = weighted + jnp.dot(
            tree_probs.astype(jnp.bfloat16), own_values, preferred_element_type=jnp.float32
        )
        return (weighted / denom_sum[:, None]).astype(jnp.bfloat16)

    return lax.map(
        per_request, (queries, tree_keys, tree_values, tree_allow, page_table, cache_len)
    )


def run_experts(rows, w_gate, w_up, w_down):
    source_count, slot_count, model_width = rows.shape
    flat_rows = rows.reshape(source_count * slot_count, model_width)
    gate_proj = jnp.dot(flat_rows, w_gate[0], preferred_element_type=jnp.float32)
    up_proj = jnp.dot(flat_rows, w_up[0], preferred_element_type=jnp.float32)
    hidden_act = (jax.nn.silu(gate_proj) * up_proj).astype(jnp.bfloat16)
    down_rows = w_down[0]
    summed = jnp.dot(
        lax.all_gather(hidden_act, "mp", axis=1, tiled=True),
        down_rows,
        preferred_element_type=jnp.float32,
    )
    outputs = summed.astype(jnp.bfloat16).reshape(source_count, slot_count, w_down.shape[2])
    return lax.all_to_all(outputs, "dp", split_axis=0, concat_axis=0, tiled=True)


def shared_experts(normed_rows, shared_gate, shared_up, shared_down):
    gate_total = jnp.dot(
        normed_rows,
        lax.all_gather(shared_gate, "dp", axis=0, tiled=True),
        preferred_element_type=jnp.float32,
    )
    up_total = jnp.dot(
        normed_rows,
        lax.all_gather(shared_up, "dp", axis=0, tiled=True),
        preferred_element_type=jnp.float32,
    )
    shared_hidden = (jax.nn.silu(gate_total) * up_total).astype(jnp.bfloat16)
    terms = jnp.dot(
        shared_hidden,
        lax.all_gather(shared_down, "dp", axis=1, tiled=True),
        preferred_element_type=jnp.float32,
    )
    return lax.psum_scatter(terms.astype(jnp.bfloat16), "mp", scatter_dimension=1, tiled=True)


def on_device(
    tree_query,
    new_kv,
    kv_cache,
    page_table,
    cache_len,
    tree_mask,
    out_weight,
    residual_in,
    norm_gain,
    route_ids,
    route_weight,
    w_gate,
    w_up,
    w_down,
    shared_gate,
    shared_up,
    shared_down,
):
    tok_rows = tree_query.shape[0]
    req_count = cache_len.shape[0]
    tree_len = tree_mask.shape[1]
    head_width = new_kv.shape[2]
    local_heads = tree_query.shape[1] // head_width
    score_scale = head_width ** (-0.5)
    queries = tree_query.reshape(req_count, tree_len, local_heads, head_width)
    queries = queries.transpose(0, 2, 1, 3).reshape(req_count, local_heads * tree_len, head_width)
    tree_keys = new_kv[:, 0, :].reshape(req_count, tree_len, head_width)
    tree_values = new_kv[:, 1, :].reshape(req_count, tree_len, head_width)
    tree_allow = jnp.tile(tree_mask, (1, local_heads, 1)) == 1
    attended = attend_requests(
        queries, tree_keys, tree_values, tree_allow, kv_cache, page_table, cache_len, score_scale
    )
    attended = attended.reshape(req_count, local_heads, tree_len, head_width).transpose(0, 2, 1, 3)
    attended = attended.reshape(tok_rows, local_heads * head_width)
    partial_value = jnp.dot(attended, out_weight, preferred_element_type=jnp.float32)
    model_width = residual_in.shape[1]
    quarter = model_width // lax.axis_size("mp")
    col_start = lax.axis_index("mp") * quarter
    experts = lax.axis_size("dp") * w_gate.shape[0]
    route_count = route_ids.shape[1]
    capacity = min(tok_rows, 4 * tok_rows * route_count // (3 * experts))
    expert_ids = route_ids.reshape(-1)
    onehot = (expert_ids[:, None] == jnp.arange(experts, dtype=jnp.int32)[None, :]).astype(
        jnp.int32
    )
    slot_index = jnp.sum((jnp.cumsum(onehot, axis=0) - onehot) * onehot, axis=1)
    sources = jnp.arange(expert_ids.shape[0], dtype=jnp.int32) // route_count
    summed_heads = lax.psum(partial_value, "mp")
    stream = (residual_in.astype(jnp.float32) + summed_heads).astype(jnp.bfloat16)
    own_stream = lax.dynamic_slice_in_dim(stream, col_start, quarter, 1)
    normed_rows = normalize(stream, norm_gain)
    buffer = jnp.zeros((experts, capacity, normed_rows.shape[1]), jnp.bfloat16)
    results = run_experts(
        lax.all_to_all(
            buffer.at[expert_ids, slot_index].set(normed_rows[sources]),
            "dp",
            split_axis=0,
            concat_axis=0,
            tiled=True,
        ),
        w_gate,
        w_up,
        w_down,
    )
    shared_out = shared_experts(normed_rows, shared_gate, shared_up, shared_down)
    result_rows = results.reshape(experts * capacity, quarter)
    picked = (
        result_rows[expert_ids * capacity + slot_index]
        .reshape(tok_rows, route_count, quarter)
        .astype(jnp.float32)
    )
    mixture = jnp.einsum("tk,tkc->tc", route_weight, picked, precision=lax.Precision.HIGHEST)
    return (own_stream.astype(jnp.float32) + shared_out.astype(jnp.float32) + mixture).astype(
        jnp.bfloat16
    )


def solution(mesh):
    return jax.shard_map(
        on_device,
        mesh=mesh,
        in_specs=(
            P("dp", "mp"),
            P("dp", None, "mp"),
            P("dp", None, None, "mp"),
            P("dp", None),
            P("dp"),
            P("dp", None, None),
            P("mp", None),
            P("dp", None),
            P(),
            P("dp", None),
            P("dp", None),
            P("dp", None, "mp"),
            P("dp", None, "mp"),
            P("dp", None, "mp"),
            P("dp", "mp"),
            P("dp", "mp"),
            P("mp", "dp"),
        ),
        out_specs=P("dp", "mp"),
        check_vma=False,
    )
```

profile of v0, /device:TPU:8, one launch (start us, length us, event | category | flops | bytes accessed | tf_op | source)
XLA Modules:
  0.0 659.3 jit_solution(10278691214841616985)
XLA Ops:
  6.5 1.1 fusion.66
  7.7 0.9 reshape.211
  8.7 0.9 broadcast_compare_fusion
  9.5 0.1 copy.21
  9.6 0.1 tile.2
  9.7 0.2 eq.37
  9.9 21.6 %while.10 = (s32[]{:T(128)}, bf16[2,256,128]{2,1,0:T(8,128)(2,1)S(1)}, s32[2]{0:T(128)}, bf16[2,256,128]{2,1,0:T(8,128)(2,1)S(1)}, s32[2,32]{1,0:T(2,128)}, /*in...) while((s32[]{:T(128)}, ...), condition=%wide.region_5.6_spmd, body=%wide.region_0.5_spmd.sunk | while | flops 554947200 | bytes 23845564 | solution.py:48
  9.9 0.7 fusion.100
  10.6 3.9 gather_fusion
  14.5 1.7 fusion.101
  16.2 0.7 dynamic_slice.79
  16.9 0.7 iota_compare_fusion.4
  17.6 0.8 fusion.102
  18.4 0.2 fusion.103
  18.6 0.9 fusion.105
  19.6 0.9 fusion.104
  20.5 0.2 fusion.107
  20.7 0.7 fusion.100
  21.4 3.9 gather_fusion
  25.3 1.7 fusion.101
  27.0 0.7 dynamic_slice.79
  27.7 0.7 iota_compare_fusion.4
  28.4 0.8 fusion.102
  29.2 0.2 fusion.103
  29.4 0.9 fusion.105
  30.4 0.9 fusion.104
  31.3 0.2 fusion.107
  31.5 0.1 copy.24
  31.7 1.5 fusion.55
  33.2 0.0 all-gather.11.cloned.1.call-start
  33.2 0.1 copy.25
  33.3 0.1 eq.42
  33.5 0.1 eq.38
  33.6 0.1 reshape.215
  33.8 1.8 reduce-window.6
  35.6 0.3 slice_reduce_fusion
  35.9 0.1 fusion.52
  36.1 51.0 %all-reduce.2.cloned.1.call-done = f32[128,2048]{1,0:T(8,128)} async-done(((f32[128,2048]{1,0:T(8,128)}), f32[128,2048]{1,0:T(8,128)}) %all-reduce.2.cloned.1.call-update) | async-done | bytes 1048592 | tf_op jit(solution)/shard_map/psum | solution.py:137
  87.1 1.5 fusion.41
  88.6 0.8 copy-done.1
  89.4 0.2 fusion.43
  89.6 4.3 gather_fusion.1
  93.9 2.4 broadcast_in_dim.47
  96.3 137.9 %scatter_fusion = bf16[64,16,2048]{2,1,0:T(8,128)(2,1)} fusion(bf16[64,16,2048]{2,1,0:T(8,128)(2,1)} %broadcast_in_dim.47, s32[768]{0:T(1024)S(1)} %get-tuple-element.54, bf16[768,2048]{1,0:T(8,128)(2,1)} %gather_fusion.1), kind=kCustom, calls=%fused_computation.3 | custom fusion | bytes 9443328 | tf_op jit(solution)/shard_map/scatter | solution.py:144
  234.3 106.9 %all_to_all.10 = bf16[64,16,2048]{2,1,0:T(8,128)(2,1)S(1)} all-to-all(bf16[64,16,2048]{2,1,0:T(8,128)(2,1)} %scatter_fusion), channel_id=1, replica_groups=mesh['dp'=64,'mp'=4] {'dp'}, dimensions={0} | all-to-all | bytes 8388608 | tf_op jit(solution)/shard_map/all_to_all | solution.py:143
  341.2 1.8 fusion.35
  343.0 2.7 fusion.37
  345.8 0.7 all-gather.5.cloned.1.call-update
  346.5 0.5 all-gather.7.cloned.1.call-update
  347.1 0.5 all-gather.9.cloned.1.call-update
  347.6 33.9 %all-gather.11.cloned.1.call-done = bf16[1024,1408]{0,1:T(8,128)(2,1)} async-done(((bf16[1024,352]{0,1:T(8,128)(2,1)}), bf16[1024,1408]{0,1:T(8,128)(2,1)}) %all-gather.11.cloned.1.call-update) | async-done | bytes 2883600 | tf_op jit(solution)/shard_map/all_gather | solution.py:61
  381.5 5.1 convolution_convert_fusion.1
  386.6 10.7 %all-to-all-start.1 = ((bf16[64,16,512]{2,1,0:T(8,128)(2,1)}), bf16[64,16,512]{2,1,0:T(8,128)(2,1)}, u32[]{:S(2)}, u32[]{:S(2)}) async-start(bf16[64,16,512]{2,1,0:T(8,128)(2,1)} %bitcast.139), calls=%async_computation.2 | async-start | bytes 2097152 | tf_op jit(solution)/shard_map/all_to_all | solution.py:66
  397.4 66.0 %all-gather.5.cloned.1.call-done = bf16[2048,704]{1,0:T(8,128)(2,1)} async-done(((bf16[32,704]{1,0:T(8,128)(2,1)}), bf16[2048,704]{1,0:T(8,128)(2,1)}) %all-gather.5.cloned.1.call-update) | async-done | bytes 2883600 | tf_op jit(solution)/shard_map/all_gather | solution.py:72
  463.4 3.2 fusion.67
  466.6 75.6 %all-gather.7.cloned.1.call-done = bf16[2048,704]{1,0:T(8,128)(2,1)} async-done(((bf16[32,704]{1,0:T(8,128)(2,1)}), bf16[2048,704]{1,0:T(8,128)(2,1)}) %all-gather.7.cloned.1.call-update) | async-done | bytes 2883600 | tf_op jit(solution)/shard_map/all_gather | solution.py:77
  542.2 78.8 %all-gather.9.cloned.1.call-done = bf16[704,2048]{0,1:T(8,128)(2,1)} async-done(((bf16[704,32]{0,1:T(8,128)(2,1)}), bf16[704,2048]{0,1:T(8,128)(2,1)}) %all-gather.9.cloned.1.call-update) | async-done | bytes 2883600 | tf_op jit(solution)/shard_map/all_gather | solution.py:83
  621.0 7.0 %convolution_convert_fusion = bf16[128,2048]{1,0:T(8,128)(2,1)} fusion(bf16[704,2048]{0,1:T(8,128)(2,1)} %all-gather.9.cloned.1.call-done, bf16[128,2048]{1,0:T(8,128)(2,1)S(1)} %fusion.43, bf16[2048,704]{1,0:T(8,128)(2,1)} %all-gather.7.cloned.1.call-done, f32[128,704]{0,1:T(8,128)S(1)} %fusion.67), kind=kOutput, calls=%fused_computation.44 | convolution fusion | flops 739000320 | bytes 7176192 | tf_op jit(solution)/shard_map/dot_general | solution.py:81
  628.1 0.1 copy.29
  628.2 4.7 gather_fusion.2
  632.9 1.3 reshape.220
  634.3 1.0 fusion.68
  635.2 15.5 %reduce-scatter.2.cloned.1.call-done = bf16[128,512]{1,0:T(8,128)(2,1)} async-done(((bf16[128,2048]{1,0:T(8,128)(2,1)}), bf16[128,512]{1,0:T(8,128)(2,1)}) %reduce-scatter.2.cloned.1.call-update) | async-done | bytes 131088 | tf_op jit(solution)/shard_map/reduce_scatter | solution.py:86
  650.8 1.7 fusion.49
  (47 shorter events, 0.5 us)
Async XLA Ops:
  6.5 25.1 %copy-start = (bf16[512,2048]{1,0:T(8,128)(2,1)S(1)}, bf16[512,2048]{1,0:T(8,128)(2,1)}, u32[]{:S(2)}) copy-start(bf16[512,2048]{1,0:T(8,128)(2,1)} %param.25) | copy-start | bytes 6291460
  6.5 80.6 %all-reduce.2.cloned.1.call-start = ((), (), s32[]{:S(2)}) async-start(), calls=%async_computation.3 | async-start | bytes 2097152 | tf_op jit(solution)/shard_map/psum | solution.py:137
  14.5 1.7 copy-start.8
  25.3 1.7 copy-start.8
  31.5 1.7 copy-start.4
  31.5 55.6 %copy-start.2 = (bf16[128,2048]{1,0:T(8,128)(2,1)S(1)}, bf16[128,2048]{1,0:T(8,128)(2,1)}, u32[]{:S(2)}) copy-start(bf16[128,2048]{1,0:T(8,128)(2,1)} %param.26) | copy-start | bytes 1572868
  31.6 57.8 %copy-start.3 = (f32[2048]{0:T(1024)S(1)}, f32[2048]{0:T(1024)}, u32[]{:S(2)}) copy-start(f32[2048]{0:T(1024)} %param.27) | copy-start | bytes 24580
  33.2 348.4 %all-gather.11.cloned.1.call-start = ((), (), s32[]{:S(2)}) async-start(), calls=%async_computation.8 | async-start | bytes 3604480 | tf_op jit(solution)/shard_map/all_gather | solution.py:61
  88.6 0.8 copy-start.1
  234.3 106.9 %copy-start.6 = (bf16[1,2048,352]{1,2,0:T(8,128)(2,1)S(1)}, bf16[1,2048,352]{1,2,0:T(8,128)(2,1)}, u32[]{:S(2)}) copy-start(bf16[1,2048,352]{1,2,0:T(8,128)(2,1)} %param.30) | copy-start | bytes 4325380
  341.2 1.8 copy-start.7
  345.7 117.7 %all-gather.5.cloned.1.call-start = ((), (), s32[]{:S(2)}) async-start(), calls=%async_computation.4 | async-start | bytes 3194880 | tf_op jit(solution)/shard_map/all_gather | solution.py:72
  346.4 195.8 %all-gather.7.cloned.1.call-start = ((), (), s32[]{:S(2)}) async-start(), calls=%async_computation.5 | async-start | bytes 3194880 | tf_op jit(solution)/shard_map/all_gather | solution.py:77
  347.0 274.0 %all-gather.9.cloned.1.call-start = ((), (), s32[]{:S(2)}) async-start(), calls=%async_computation.6 | async-start | bytes 3194880 | tf_op jit(solution)/shard_map/all_gather | solution.py:83
  386.6 241.6 %all-to-all-start.1 = ((bf16[64,16,512]{2,1,0:T(8,128)(2,1)}), bf16[64,16,512]{2,1,0:T(8,128)(2,1)}, u32[]{:S(2)}, u32[]{:S(2)}) async-start(bf16[64,16,512]{2,1,0:T(8,128)(2,1)} %bitcast.139), calls=%async_computation.2 | async-start | bytes 2097152 | tf_op jit(solution)/shard_map/all_to_all | solution.py:66
  397.4 253.4 %reduce-scatter.2.cloned.1.call-start = ((), (), s32[]{:S(2)}) async-start(), calls=%async_computation.7 | async-start | bytes 655360 | tf_op jit(solution)/shard_map/reduce_scatter | solution.py:86
  466.6 161.4 %copy-start.5 = (f32[128,6]{0,1:T(8,128)S(1)}, f32[128,6]{0,1:T(8,128)}, u32[]{:S(2)}) copy-start(f32[128,6]{0,1:T(8,128)} %param.29) | copy-start | bytes 9220
Sparse Core Ops, SparseCore 0:
  33.3 53.8 all-reduce.1
  345.8 35.6 all-gather.10
  384.7 78.7 all-gather.4
  466.4 75.7 all-gather.6
  545.2 75.7 all-gather.8
  628.2 22.5 reduce-scatter.1
where the time goes:
time: 663 us; the launch traced here: 659 us
  waiting for transfers between devices  323 us (49%)
  local copies, waits for them, and re-layouts  168 us (25%)
  blocking collectives  107 us (16%)
  matrix products  26.4 us (4%)
  between operations  13.7 us (2%)
  starting transfers between devices  10.9 us (2%)
  other arithmetic  10.9 us (2%)
    scatter x1, local copies, waits for them, and re-layouts, on_device(): buffer.at[expert_ids, slot_index].set(normed_rows[sources])  138 us
    all_to_all x1, blocking collectives, on_device(): lax.all_to_all(buffer.at[expert_ids, slot_index].set(normed_rows[sources]...  107 us
    all_gather x1, waiting for transfers between devices, shared_experts(): lax.all_gather(shared_down, 'dp', axis=1, tiled=True)  78.8 us
    all_gather x1, waiting for transfers between devices, shared_experts(): lax.all_gather(shared_up, 'dp', axis=0, tiled=True)  75.6 us
    all_gather x1, waiting for transfers between devices, shared_experts(): lax.all_gather(shared_gate, 'dp', axis=0, tiled=True)  66 us
    psum x1, waiting for transfers between devices, on_device(): summed_heads = lax.psum(partial_value, 'mp')  51 us
    all_gather x1, waiting for transfers between devices, run_experts(): lax.all_gather(hidden_act, 'mp', axis=1, tiled=True)  33.9 us
    reduce_scatter x1, waiting for transfers between devices, shared_experts(): lax.psum_scatter(terms.astype(jnp.bfloat16), 'mp', scatter_dimension=1, t...  15.5 us
  transfers between devices with their start and end apart: 7, of which 6 were waited for; matrix products, arithmetic and copies ran while one was open for 4% of the time, Pallas kernels for 0%

commit v1 on v0

--- a/solution.py
+++ b/solution.py
@@ -5,6 +5,24 @@
 
 NEGATIVE_FILL = -1e30
 EPSILON = 1e-05
+
+
+def collect(shard, axis, dim):
+    ways, here, hop = (lax.axis_size(axis), lax.axis_index(axis), shard.shape[dim])
+    shape = [n * ways if d == dim else n for d, n in enumerate(shard.shape)]
+    full = lax.dynamic_update_slice_in_dim(
+        jnp.zeros(shape, shard.dtype), shard, here * hop, axis=dim
+    )
+    going_up = going_down = shard
+    for far in range(1, ways // 2 + 1):
+        going_up = lax.ppermute(going_up, axis, [(d, (d + 1) % ways) for d in range(ways)])
+        full = lax.dynamic_update_slice_in_dim(full, going_up, (here - far) % ways * hop, axis=dim)
+        if 2 * far < ways:
+            going_down = lax.ppermute(going_down, axis, [(d, (d - 1) % ways) for d in range(ways)])
+            full = lax.dynamic_update_slice_in_dim(
+                full, going_down, (here + far) % ways * hop, axis=dim
+            )
+    return full
 
 
 def normalize(rows, gain):
@@ -57,11 +75,7 @@
     up_proj = jnp.dot(flat_rows, w_up[0], preferred_element_type=jnp.float32)
     hidden_act = (jax.nn.silu(gate_proj) * up_proj).astype(jnp.bfloat16)
     down_rows = w_down[0]
-    summed = jnp.dot(
-        lax.all_gather(hidden_act, "mp", axis=1, tiled=True),
-        down_rows,
-        preferred_element_type=jnp.float32,
-    )
+    summed = jnp.dot(collect(hidden_act, "mp", 1), down_rows, preferred_element_type=jnp.float32)
     outputs = summed.astype(jnp.bfloat16).reshape(source_count, slot_count, w_down.shape[2])
     return lax.all_to_all(outputs, "dp", split_axis=0, concat_axis=0, tiled=True)
 

time: 663 us -> 466 us (0.70)
  waiting for transfers between devices: 323 us -> 205 us
  blocking collectives: 107 us -> 0 us
  starting transfers between devices: 10.9 us -> 25.1 us
    all_to_all x1 -> x0, blocking collectives: 107 us -> none  [on_device(): lax.all_to_all(buffer.at[expert_ids, slot_index].set(normed_rows[sources]...]
    all_to_all x0 -> x1, waiting for transfers between devices: none -> 104 us  [on_device(): lax.all_to_all(buffer.at[expert_ids, slot_index].set(normed_rows[sources]...]
    all_gather x1, waiting for transfers between devices: 75.6 us -> 0.03 us  [shared_experts(): lax.all_gather(shared_up, 'dp', axis=0, tiled=True)]
    all_gather x1, waiting for transfers between devices: 78.8 us -> 5.13 us  [shared_experts(): lax.all_gather(shared_down, 'dp', axis=1, tiled=True)]
    all_gather x1, waiting for transfers between devices: 66 us -> 0.03 us  [shared_experts(): lax.all_gather(shared_gate, 'dp', axis=0, tiled=True)]
    all_gather x1 -> x0, waiting for transfers between devices: 33.9 us -> none  [run_experts(): lax.all_gather(hidden_act, 'mp', axis=1, tiled=True)]
    ppermute x0 -> x3, waiting for transfers between devices: none -> 27.7 us  [the longest x2 27.7 us: collect(): lax.ppermute(going_up, axis, [(d, (d + 1) % ways) for d in range(ways)])]
    all_to_all x1, waiting for transfers between devices: 0.01 us -> 12.9 us  [run_experts(): lax.all_to_all(outputs, 'dp', split_axis=0, concat_axis=0, tiled=True)]
  transfers between devices with their start and end apart: 7 -> 10, of which waited for: 6 -> 7; matrix products, arithmetic and copies ran while one was open for 4% -> 41% of each run, Pallas kernels for 0% -> 0%
where the time goes in v1:
time: 466 us; the launch traced here: 462 us
  waiting for transfers between devices  205 us (44%)
  local copies, waits for them, and re-layouts  174 us (37%)
  matrix products  32.2 us (7%)
  starting transfers between devices  25.1 us (5%)
  between operations  15.3 us (3%)
  other arithmetic  10.9 us (2%)
    scatter x1, local copies, waits for them, and re-layouts, on_device(): buffer.at[expert_ids, slot_index].set(normed_rows[sources])  138 us
    all_to_all x1, waiting for transfers between devices, on_device(): lax.all_to_all(buffer.at[expert_ids, slot_index].set(normed_rows[sources]...  104 us
    psum x1, waiting for transfers between devices, on_device(): summed_heads = lax.psum(partial_value, 'mp')  50.5 us
    ppermute x2, waiting for transfers between devices, collect(): lax.ppermute(going_up, axis, [(d, (d + 1) % ways) for d in range(ways)])  27.7 us
    all_to_all x1, waiting for transfers between devices, run_experts(): lax.all_to_all(outputs, 'dp', split_axis=0, concat_axis=0, tiled=True)  12.9 us
    all_to_all x1, starting transfers between devices, on_device(): lax.all_to_all(buffer.at[expert_ids, slot_index].set(normed_rows[sources]...  10.8 us
    all_to_all x1, starting transfers between devices, run_experts(): lax.all_to_all(outputs, 'dp', split_axis=0, concat_axis=0, tiled=True)  10.4 us
  transfers between devices with their start and end apart: 10, of which 7 were waited for; matrix products, arithmetic and copies ran while one was open for 41% of the time, Pallas kernels for 0%

profile of v1, /device:TPU:8, one launch (start us, length us, event | category | flops | bytes accessed | tf_op | source)
XLA Modules:
  0.0 462.5 jit_solution(6194612432282783075)
XLA Ops:
  7.4 1.1 fusion.66
  8.5 0.9 reshape.211
  9.5 0.9 broadcast_compare_fusion
  10.6 0.2 eq.41
  10.7 21.6 %while.10 = (s32[]{:T(128)}, bf16[2,256,128]{2,1,0:T(8,128)(2,1)S(1)}, s32[2]{0:T(128)}, bf16[2,256,128]{2,1,0:T(8,128)(2,1)S(1)}, s32[2,32]{1,0:T(2,128)}, /*in...) while((s32[]{:T(128)}, ...), condition=%wide.region_5.6_spmd, body=%wide.region_0.5_spmd.sunk | while | flops 554947200 | bytes 23845564 | solution.py:66
  10.7 0.7 fusion.100
  11.4 3.9 gather_fusion
  15.3 1.7 fusion.101
  17.0 0.7 dynamic_slice.79
  17.7 0.7 iota_compare_fusion.4
  18.4 0.8 fusion.102
  19.2 0.2 fusion.103
  19.4 0.9 fusion.105
  20.4 0.9 fusion.104
  21.3 0.2 fusion.107
  21.5 0.7 fusion.100
  22.2 3.9 gather_fusion
  26.1 1.7 fusion.101
  27.8 0.7 dynamic_slice.79
  28.5 0.7 iota_compare_fusion.4
  29.2 0.8 fusion.102
  30.1 0.2 fusion.103
  30.2 0.9 fusion.105
  31.2 0.9 fusion.104
  32.1 0.2 fusion.107
  32.5 1.5 fusion.55
  34.0 0.5 all-gather.4.cloned.1.call-update
  35.0 0.1 reshape.215
  35.1 1.8 reduce-window.6
  36.9 0.3 slice_reduce_fusion
  37.5 50.5 %all-reduce.2.cloned.1.call-done = f32[128,2048]{1,0:T(8,128)} async-done(((f32[128,2048]{1,0:T(8,128)}), f32[128,2048]{1,0:T(8,128)}) %all-reduce.2.cloned.1.call-update) | async-done | bytes 1048592 | tf_op jit(solution)/shard_map/psum | solution.py:151
  87.9 1.5 fusion.41
  89.4 0.8 copy-done.1
  90.2 0.2 fusion.43
  90.4 4.3 gather_fusion.1
  94.7 2.5 broadcast_in_dim.51
  97.2 137.9 %scatter_fusion = bf16[64,16,2048]{2,1,0:T(8,128)(2,1)} fusion(bf16[64,16,2048]{2,1,0:T(8,128)(2,1)} %broadcast_in_dim.51, s32[768]{0:T(1024)S(1)} %get-tuple-element.54, bf16[768,2048]{1,0:T(8,128)(2,1)} %gather_fusion.1), kind=kCustom, calls=%fused_computation.3 | custom fusion | bytes 9443328 | tf_op jit(solution)/shard_map/scatter | solution.py:158
  235.1 10.8 %all-to-all-start = ((bf16[64,16,2048]{2,1,0:T(8,128)(2,1)}), bf16[64,16,2048]{2,1,0:T(8,128)(2,1)}, u32[]{:S(2)}, u32[]{:S(2)}) async-start(bf16[64,16,2048]{2,1,0:T(8,128)(2,1)} %scatter_fusion), calls=%async_computation.1 | async-start | bytes 8388608 | tf_op jit(solution)/shard_map/all_to_all | solution.py:157
  245.9 0.5 all-gather.6.cloned.1.call-update
  246.5 0.2 all-gather.8.cloned.1.call-start
  246.7 0.3 all-gather.8.cloned.1.call-update
  247.1 104.2 %all-to-all-done = bf16[64,16,2048]{2,1,0:T(8,128)(2,1)} async-done(((bf16[64,16,2048]{2,1,0:T(8,128)(2,1)}), bf16[64,16,2048]{2,1,0:T(8,128)(2,1)}, u32[]{:S(2)}, u32[]{:S(2)}) %all-to-all-start) | async-done | bytes 4194336 | tf_op jit(solution)/shard_map/all_to_all | solution.py:157
  351.2 4.3 fusion.35
  355.6 2.0 broadcast_in_dim.50
  357.5 5.2 %constant_dynamic-update-slice_fusion.3 = (bf16[1024,1408]{0,1:T(8,128)(2,1)}, bf16[1024,352]{0,1:T(8,128)(2,1)}) fusion(bf16[1024,1408]{0,1:T(8,128)(2,1)} %broadcast_in_dim.50, s32[]{:T(128)S(6)} %select_n.111, bf16[1024,2048]{1,0:T(8,128)(2,1)} %bitcast.17, bf16[1,2048,352]{1,2,0:T(8,128)(2,1)S(1)} %copy-done.6, f32[1024,352]{0,1:T(8,128)S(1)} %fusion.35), kind=kOutput, calls=%fused_computation.101 | convolution fusion | flops 1478557696 | bytes 8519684 | tf_op jit(solution)/shard_map/dot_general | solution.py:75
  362.7 0.7 collective-permute-start
  363.4 2.5 collective-permute-start.1
  365.9 14.2 %collective-permute-done = bf16[1024,352]{0,1:T(8,128)(2,1)S(1)} collective-permute-done((bf16[1024,352]{0,1:T(8,128)(2,1)}, bf16[1024,352]{0,1:T(8,128)(2,1)S(1)}, u32[]{:S(2)}, u32[]{:S(2)}) %collective-permute-start) | collective-permute-done | bytes 720928 | tf_op jit(solution)/shard_map/ppermute | solution.py:18
  380.1 0.9 constant_dynamic-update-slice_fusion.2
  381.1 2.0 constant_dynamic-update-slice_fusion.1
  383.1 13.5 %collective-permute-done.2 = bf16[1024,352]{0,1:T(8,128)(2,1)} collective-permute-done((bf16[1024,352]{0,1:T(8,128)(2,1)S(1)}, bf16[1024,352]{0,1:T(8,128)(2,1)}, u32[]{:S(2)}, u32[]{:S(2)}) %collective-permute-start.2) | collective-permute-done | bytes 720928 | tf_op jit(solution)/shard_map/ppermute | solution.py:18
  396.5 2.0 constant_dynamic-update-slice_fusion
  398.6 4.6 convolution_convert_fusion.1
  403.2 10.4 %all-to-all-start.1 = ((bf16[64,16,512]{2,1,0:T(8,128)(2,1)}), bf16[64,16,512]{2,1,0:T(8,128)(2,1)}, u32[]{:S(2)}, u32[]{:S(2)}) async-start(bf16[64,16,512]{2,1,0:T(8,128)(2,1)} %bitcast.139), calls=%async_computation.2 | async-start | bytes 2097152 | tf_op jit(solution)/shard_map/all_to_all | solution.py:80
  413.6 0.3 reduce-scatter.2.cloned.1.call-start
  413.9 3.2 fusion.67
  417.2 5.1 %all-gather.8.cloned.1.call-done = bf16[704,2048]{0,1:T(8,128)(2,1)} async-done(((bf16[704,32]{0,1:T(8,128)(2,1)}), bf16[704,2048]{0,1:T(8,128)(2,1)}) %all-gather.8.cloned.1.call-update) | async-done | bytes 2883600 | tf_op jit(solution)/shard_map/all_gather | solution.py:97
  422.3 7.0 %convolution_convert_fusion = bf16[128,2048]{1,0:T(8,128)(2,1)} fusion(bf16[704,2048]{0,1:T(8,128)(2,1)} %all-gather.8.cloned.1.call-done, bf16[128,2048]{1,0:T(8,128)(2,1)S(1)} %fusion.43, bf16[2048,704]{1,0:T(8,128)(2,1)} %all-gather.6.cloned.1.call-done, f32[128,704]{0,1:T(8,128)S(1)} %fusion.67), kind=kOutput, calls=%fused_computation.44 | convolution fusion | flops 739000320 | bytes 7176192 | tf_op jit(solution)/shard_map/dot_general | solution.py:95
  429.5 12.9 %all-to-all-done.1 = bf16[64,16,512]{2,1,0:T(8,128)(2,1)} async-done(((bf16[64,16,512]{2,1,0:T(8,128)(2,1)}), bf16[64,16,512]{2,1,0:T(8,128)(2,1)}, u32[]{:S(2)}, u32[]{:S(2)}) %all-to-all-start.1) | async-done | bytes 1048608 | tf_op jit(solution)/shard_map/all_to_all | solution.py:80
  442.4 4.1 gather_fusion.2
  446.4 1.2 reshape.220
  447.7 2.2 fusion.68
  449.9 3.3 reduce-scatter.2.cloned.1.call-done
  453.2 1.7 fusion.49
  (55 shorter events, 1.4 us)
Async XLA Ops:
  7.4 25.1 %copy-start = (bf16[512,2048]{1,0:T(8,128)(2,1)S(1)}, bf16[512,2048]{1,0:T(8,128)(2,1)}, u32[]{:S(2)}) copy-start(bf16[512,2048]{1,0:T(8,128)(2,1)} %param.25) | copy-start | bytes 6291460
  7.4 80.6 %all-reduce.2.cloned.1.call-start = ((), (), s32[]{:S(2)}) async-start(), calls=%async_computation.3 | async-start | bytes 2097152 | tf_op jit(solution)/shard_map/psum | solution.py:151
  15.3 1.7 copy-start.8
  26.1 1.7 copy-start.8
  32.3 2.2 copy-start.4
  32.5 55.5 %copy-start.2 = (bf16[128,2048]{1,0:T(8,128)(2,1)S(1)}, bf16[128,2048]{1,0:T(8,128)(2,1)}, u32[]{:S(2)}) copy-start(bf16[128,2048]{1,0:T(8,128)(2,1)} %param.26) | copy-start | bytes 1572868
  34.0 56.2 %copy-start.3 = (f32[2048]{0:T(1024)S(1)}, f32[2048]{0:T(1024)}, u32[]{:S(2)}) copy-start(f32[2048]{0:T(1024)} %param.27) | copy-start | bytes 24580
  34.0 379.9 %all-gather.4.cloned.1.call-start = ((), (), s32[]{:S(2)}) async-start(), calls=%async_computation.4 | async-start | bytes 3194880 | tf_op jit(solution)/shard_map/all_gather | solution.py:86
  89.4 0.8 copy-start.1
  235.1 116.2 %all-to-all-start = ((bf16[64,16,2048]{2,1,0:T(8,128)(2,1)}), bf16[64,16,2048]{2,1,0:T(8,128)(2,1)}, u32[]{:S(2)}, u32[]{:S(2)}) async-start(bf16[64,16,2048]{2,1,0:T(8,128)(2,1)} %scatter_fusion), calls=%async_computation.1 | async-start | bytes 8388608 | tf_op jit(solution)/shard_map/all_to_all | solution.py:157
  245.9 171.3 %all-gather.6.cloned.1.call-start = ((), (), s32[]{:S(2)}) async-start(), calls=%async_computation.5 | async-start | bytes 3194880 | tf_op jit(solution)/shard_map/all_gather | solution.py:91
  246.5 175.8 %all-gather.8.cloned.1.call-start = ((), (), s32[]{:S(2)}) async-start(), calls=%async_computation.6 | async-start | bytes 3194880 | tf_op jit(solution)/shard_map/all_gather | solution.py:97
  355.5 2.0 copy-start.6
  362.7 17.4 %collective-permute-start = (bf16[1024,352]{0,1:T(8,128)(2,1)}, bf16[1024,352]{0,1:T(8,128)(2,1)S(1)}, u32[]{:S(2)}, u32[]{:S(2)}) collective-permute-start(bf16[1024,352]{0,1:T(8,128)(2,1)} %get-tuple-element.84), channel_id=1, source_target_pairs={{0,1},{1,2},{2,3},{3,0},{4,5},{5,6},{6,7},{7,4},{8,9},{9,10},{10,1... | collective-permute-start | bytes 2162696 | tf_op jit(solution)/shard_map/ppermute | solution.py:18
  363.4 17.7 %collective-permute-start.1 = (bf16[1024,352]{0,1:T(8,128)(2,1)}, bf16[1024,352]{0,1:T(8,128)(2,1)}, u32[]{:S(2)}, u32[]{:S(2)}) collective-permute-start(bf16[1024,352]{0,1:T(8,128)(2,1)} %get-tuple-element.84), channel_id=1, source_target_pairs={{0,3},{1,0},{2,1},{3,2},{4,7},{5,4},{6,5},{7,6},{8,11},{9,8},{10,9... | collective-permute-start | bytes 2162696 | tf_op jit(solution)/shard_map/ppermute | solution.py:21
  380.1 16.4 %collective-permute-start.2 = (bf16[1024,352]{0,1:T(8,128)(2,1)S(1)}, bf16[1024,352]{0,1:T(8,128)(2,1)}, u32[]{:S(2)}, u32[]{:S(2)}) collective-permute-start(bf16[1024,352]{0,1:T(8,128)(2,1)S(1)} %collective-permute-done), channel_id=1, source_target_pairs={{0,1},{1,2},{2,3},{3,0},{4,5},{5,6},{6,7},{7,4},{8,9},{9,10},{10,1... | collective-permute-start | bytes 2162696 | tf_op jit(solution)/shard_map/ppermute | solution.py:18
  380.1 18.4 %copy-start.7 = (bf16[1,1408,512]{2,1,0:T(8,128)(2,1)S(1)}, bf16[1,1408,512]{2,1,0:T(8,128)(2,1)}, u32[]{:S(2)}) copy-start(bf16[1,1408,512]{2,1,0:T(8,128)(2,1)} %param.32) | copy-start | bytes 4325380
  403.2 39.2 %all-to-all-start.1 = ((bf16[64,16,512]{2,1,0:T(8,128)(2,1)}), bf16[64,16,512]{2,1,0:T(8,128)(2,1)}, u32[]{:S(2)}, u32[]{:S(2)}) async-start(bf16[64,16,512]{2,1,0:T(8,128)(2,1)} %bitcast.139), calls=%async_computation.2 | async-start | bytes 2097152 | tf_op jit(solution)/shard_map/all_to_all | solution.py:80
  413.6 39.6 %reduce-scatter.2.cloned.1.call-start = ((), (), s32[]{:S(2)}) async-start(), calls=%async_computation.7 | async-start | bytes 655360 | tf_op jit(solution)/shard_map/reduce_scatter | solution.py:100
  417.1 12.2 %copy-start.5 = (f32[128,6]{0,1:T(8,128)S(1)}, f32[128,6]{0,1:T(8,128)}, u32[]{:S(2)}) copy-start(f32[128,6]{0,1:T(8,128)} %param.29) | copy-start | bytes 9220
Sparse Core Ops, SparseCore 0:
  34.1 53.7 all-reduce.1
  429.5 23.7 reduce-scatter.1
Sparse Core Ops, SparseCore 1:
  37.6 80.1 all-gather.3
  249.5 92.7 all-gather.5
  345.2 77.0 all-gather.7
